TPU v7x, 256 devices: a whole 4x4x8 slice. The times are simulated.
256 devices in a mesh: blk: 32 (over z, y_lo, core), grp: 8 (over x, y_hi).
Axes of the slice: x: 4, y: 4 (y_hi: 2, y_lo: 2; y = y_hi * 2 + y_lo), z: 8, core: 2. Of those that a mesh axis runs over, the one named last changes fastest.
Arguments:
- low_sites: float32 [8, 32768], P(None, ('blk', 'grp')), may hold values from -6 to 6
- low_probes: float32 [8, 32768], P(None, ('blk', 'grp')), may hold values from -0.03314563 to 0.03314563
- high_probes: float32 [8, 16384], P(None, ('blk', 'grp')), may hold values from -0.03314563 to 0.03314563
- nested: int32 [16384], P(('blk', 'grp')), may hold values from 0 to 32767, as said below
- inv_len_low: float32 [8], replicated, may hold values from 0.15 to 0.6
- inv_len_diff: float32 [8], replicated, may hold values from 0.2 to 0.8
Outputs:
- low_out: float32 [8, 32768], P(None, ('blk', 'grp'))
- high_out: float32 [8, 16384], P(None, ('blk', 'grp'))
Inputs may be any that keep to these rules, and one draw needn't show every extreme that they name: `nested`: entries are distinct; the high sites in the aligned block of 512 entries number b all lie among the low sites b * 1024 to (b + 1) * 1024 - 1.
All inputs are finite; a program needn't handle non-finite values.
Results may differ from a plain program's by a relative error of at most 0.00021.
Values sent between devices are 32-bit elements; how exact they have to be, the bound alone decides.
No kernel may reach another device: no remote copies, remote signals or barrier semaphores. Data moves between devices by JAX's collectives and lax.ppermute only.
A program may use at most 64 MiB of HBM per device.

v0:
```python
import math
import jax
import jax.numpy as jnp
from jax import lax
from jax.sharding import PartitionSpec as P

RHO = 0.9
VAR_DIFF = 1.0
SQRT_THREE = 1.7320508075688772


def matern(rows, cols):
    inner = jnp.einsum("fr,fc->rc", rows, cols, precision=lax.Precision.HIGHEST)
    square = jnp.sum(rows * rows, 0)[:, None] + jnp.sum(cols * cols, 0)[None, :] - 2.0 * inner
    dist = jnp.sqrt(jnp.maximum(square, 0.0))
    return (1.0 + SQRT_THREE * dist) * jnp.exp(-SQRT_THREE * dist)


def partial_product(rows, cols, weights):
    tile = matern(rows, cols)
    return jnp.einsum("pc,rc->pr", weights, tile, precision=lax.Precision.HIGHEST)


def apply_blocked(rows, cols, weights):
    count = cols.shape[1]
    step = math.gcd(count, 2048)
    blocks = count // step
    cols_split = cols.reshape(cols.shape[0], blocks, step).transpose(1, 0, 2)
    weights_split = weights.reshape(weights.shape[0], blocks, step).transpose(1, 0, 2)

    def one_block(total, item):
        return (total + partial_product(rows, item[0], item[1]), None)

    start = jnp.zeros((weights.shape[0], rows.shape[1]), jnp.float32)
    total, _ = lax.scan(one_block, start, (cols_split, weights_split))
    return total


def per_device(low_sites, low_probes, high_probes, nested, inv_len_low, inv_len_diff):
    rows_dev = low_sites.shape[1]
    feats_block, lowp_block, highp_block = (
        lax.all_gather(low_sites, "grp", axis=1, tiled=True),
        lax.all_gather(low_probes, "grp", axis=1, tiled=True),
        lax.all_gather(high_probes, "grp", axis=1, tiled=True),
    )
    nest_block = lax.all_gather(nested, "grp", axis=0, tiled=True)
    width = feats_block.shape[1]
    base = lax.axis_index("blk") * width
    place_block = nest_block - base
    own_place = nested - base
    slots = lax.broadcasted_iota(jnp.int32, (width,), 0)
    pick_own = (slots[:, None] == own_place[None, :]).astype(jnp.float32)
    high_feats = jnp.dot(
        feats_block, pick_own, precision=lax.Precision.HIGHEST, preferred_element_type=jnp.float32
    )
    rows_low = low_sites * inv_len_low[:, None]
    rows_diff = high_feats * inv_len_diff[:, None]
    own_slots = lax.axis_index("grp") * rows_dev + lax.broadcasted_iota(jnp.int32, (rows_dev,), 0)
    spread_own = (place_block[:, None] == own_slots[None, :]).astype(jnp.float32)
    mixed_own = low_probes + RHO * jnp.dot(
        highp_block, spread_own, precision=lax.Precision.HIGHEST, preferred_element_type=jnp.float32
    )
    cols_feat = lax.all_gather(low_sites, ("blk", "grp"), axis=1, tiled=True)
    cols_weight = lax.all_gather(mixed_own, ("blk", "grp"), axis=1, tiled=True)
    cols_high = lax.all_gather(high_feats, ("blk", "grp"), axis=1, tiled=True)
    cols_hprobe = lax.all_gather(high_probes, ("blk", "grp"), axis=1, tiled=True)
    low_cols = cols_feat * inv_len_low[:, None]
    new_low = apply_blocked(rows_low, low_cols, cols_weight)
    new_diff = VAR_DIFF * apply_blocked(rows_diff, cols_high * inv_len_diff[:, None], cols_hprobe)
    low_block = lax.all_gather(new_low, "grp", axis=1, tiled=True)
    high_part = jnp.dot(
        low_block, pick_own, precision=lax.Precision.HIGHEST, preferred_element_type=jnp.float32
    )
    high_out = RHO * high_part + new_diff
    return (new_low, high_out)


def solution(mesh):
    return jax.shard_map(
        per_device,
        mesh=mesh,
        in_specs=(
            P(None, ("blk", "grp")),
            P(None, ("blk", "grp")),
            P(None, ("blk", "grp")),
            P(("blk", "grp")),
            P(),
            P(),
        ),
        out_specs=(P(None, ("blk", "grp")), P(None, ("blk", "grp"))),
        check_vma=False,
    )
```

profile of v0, /device:TPU:128, one launch (start us, length us, event | category | flops | bytes accessed | tf_op | source)
XLA Modules:
  0.0 1467.7 jit_solution(3234751607387825071)
XLA Ops:
  8.0 34.4 %all-gather = f32[8,64,8]{1,2,0:T(8,128)S(1)} all-gather(f32[1,64,8]{1,2,0:T(8,128)S(1)} %bitcast.97), channel_id=1, replica_groups=mesh['blk'=32,'grp'=8] {'grp'}, dimensions={0}, use_global_device_ids=true | all-gather | bytes 18432 | tf_op jit(solution)/shard_map/all_gather | solution.py:44
  45.2 12.8 all-reduce
  60.2 34.3 %all_gather.30 = f32[8,1024]{1,0:T(8,128)S(1)} all-gather(f32[8,128]{1,0:T(8,128)S(1)} %copy-done), channel_id=1, replica_groups=mesh['blk'=32,'grp'=8] {'grp'}, dimensions={1}, use_global_device_ids=true | all-gather | bytes 36864 | tf_op jit(solution)/shard_map/all_gather | solution.py:42
  94.5 626.2 %all-gather.1 = f32[256,64,8]{1,2,0:T(8,128)S(1)} all-gather(f32[1,64,8]{1,2,0:T(8,128)S(1)} %bitcast.98), channel_id=1, replica_groups=mesh['blk'=32,'grp'=8] {'blk','grp'}, dimensions={0}, use_global_device_ids=true | all-gather | bytes 526336 | tf_op jit(solution)/shard_map/all_gather | solution.py:66
  721.1 627.4 %all-gather.2 = f32[256,64,8]{1,2,0:T(8,128)S(1)} all-gather(f32[1,64,8]{1,2,0:T(8,128)S(1)} %bitcast.99), channel_id=1, replica_groups=mesh['blk'=32,'grp'=8] {'blk','grp'}, dimensions={0}, use_global_device_ids=true | all-gather | bytes 526336 | tf_op jit(solution)/shard_map/all_gather | solution.py:65
  1350.7 12.1 while.27
  1364.2 61.5 %while.26 = (s32[]{:T(128)}, f32[8,128]{1,0:T(8,128)S(1)}, f32[16,8,2048]{2,1,0:T(8,128)}, f32[128]{0:T(128)S(1)}, f32[16,8,2048]{2,1,0:T(8,128)S(1)}, /*index=5*/f32[8,128]{1,0:T(8,128)S(1)}, s32[]{:T(128)}, s32[]{:T(128)}) while((s32[]{:T(128)}, f32[8,128]{1,0:T(8,128)S(1)}, f32[16,8,2048]{2,1,0:T(8,128)}, f32[128]{0:T(128)S(1)}, ...), condition=%wide.region_3.4_spmd.clone, body=%wide.region_1.3_spmd.clone.sunk | while | flops 52461568 | bytes 2323059 | solution.py:35
  1364.3 2.1 fusion.65
  1368.1 2.1 fusion.65
  1372.0 2.1 fusion.65
  1375.8 2.1 fusion.65
  1379.6 2.1 fusion.65
  1383.5 2.1 fusion.65
  1387.3 2.1 fusion.65
  1391.2 2.1 fusion.65
  1395.0 2.1 fusion.65
  1398.8 2.1 fusion.65
  1402.7 2.1 fusion.65
  1406.5 2.1 fusion.65
  1410.4 2.1 fusion.65
  1414.2 2.1 fusion.65
  1418.1 2.1 fusion.65
  1421.9 2.1 fusion.65
  1425.7 34.3 %all_gather.28 = f32[8,1024]{1,0:T(8,128)S(1)} all-gather(f32[8,128]{1,0:T(8,128)S(1)} %get-tuple-element.132), channel_id=1, replica_groups=mesh['blk'=32,'grp'=8] {'grp'}, dimensions={1}, use_global_device_ids=true | all-gather | bytes 36864 | tf_op jit(solution)/shard_map/all_gather | solution.py:70
  (108 shorter events, 48.5 us)
Async XLA Ops:
  7.2 0.8 copy-start.1
  7.2 1355.6 %all-gather.8.cloned.1.call-start = ((), (), s32[]{:S(2)}) async-start(), calls=%async_computation.1 | async-start | bytes 1052672 | tf_op jit(solution)/shard_map/all_gather | solution.py:63
  7.9 1356.3 %all-gather.6.cloned.1.call-start = ((), (), s32[]{:S(2)}) async-start(), calls=%async_computation | async-start | bytes 1052672 | tf_op jit(solution)/shard_map/all_gather | solution.py:64
  42.4 0.7 copy-start.7
  44.3 0.7 copy-start.6
  57.9 0.7 copy-start.5
  59.5 0.7 copy-start
  94.5 626.2 %copy-start.4 = (f32[8]{0:T(128)S(1)}, f32[8]{0:T(128)}, u32[]{:S(2)}) copy-start(f32[8]{0:T(128)} %param.14) | copy-start | bytes 100
  1348.7 0.7 copy-start.3
  1425.7 34.3 %copy-start.2 = (f32[8,128]{1,0:T(8,128)}, f32[8,128]{1,0:T(8,128)S(1)}, u32[]{:S(2)}) copy-start(f32[8,128]{1,0:T(8,128)S(1)} %get-tuple-element.132) | copy-start | bytes 12292
Sparse Core Ops, SparseCore 0:
  9.8 546.0 all-gather.7
  558.2 541.7 all-gather.5
where the time goes:
time: 1470 us
  blocking collectives  1370 us (93%)
  matrix products  73 us (5%)
  between operations  14.8 us (1%)
    all_gather x1, blocking collectives, per_device(): cols_high = lax.all_gather(high_feats, ('blk', 'grp'), axis=1, tiled=True)  627 us
    all_gather x1, blocking collectives, per_device(): lax.all_gather(high_probes, ('blk', 'grp'), axis=1, tiled=True)  626 us
    dot_general x24, matrix products, matern(): inner = jnp.einsum('fr,fc->rc', rows, cols, precision=lax.Precision.HIGHEST)  40.2 us
    all_gather x1, blocking collectives, per_device(): lax.all_gather(high_probes, 'grp', axis=1, tiled=True)  34.4 us
    all_gather x1, blocking collectives, per_device(): low_block = lax.all_gather(new_low, 'grp', axis=1, tiled=True)  34.3 us
    all_gather x1, blocking collectives, per_device(): lax.all_gather(low_sites, 'grp', axis=1, tiled=True)  34.3 us
    dot_general x24, matrix products, partial_product(): jnp.einsum('pc,rc->pr', weights, tile, precision=lax.Precision.HIGHEST)  30.7 us
  transfers between devices with their start and end apart: 2, of which 0 were waited for; matrix products, arithmetic and copies ran while one was open for 1% of the time, Pallas kernels for 0%

commit v1 on v0

--- a/solution.py
+++ b/solution.py
@@ -62,7 +62,12 @@
     )
     cols_feat = lax.all_gather(low_sites, ("blk", "grp"), axis=1, tiled=True)
     cols_weight = lax.all_gather(mixed_own, ("blk", "grp"), axis=1, tiled=True)
-    cols_high = lax.all_gather(high_feats, ("blk", "grp"), axis=1, tiled=True)
+    cols_high = jnp.concatenate(
+        lax.all_to_all(
+            jnp.stack([high_feats] * lax.axis_size(("blk", "grp"))), ("blk", "grp"), 0, 0
+        ),
+        axis=1,
+    )
     cols_hprobe = lax.all_gather(high_probes, ("blk", "grp"), axis=1, tiled=True)
     low_cols = cols_feat * inv_len_low[:, None]
     new_low = apply_blocked(rows_low, low_cols, cols_weight)

time: 1470 us -> 1200 us (0.82)
  blocking collectives: 1370 us -> 744 us
  waiting for transfers between devices: 0.74 us -> 339 us
    all_gather x1 -> x0, blocking collectives: 627 us -> none  [per_device(): cols_high = lax.all_gather(high_feats, ('blk', 'grp'), axis=1, tiled=True)]
    all_gather x1, waiting for transfers between devices: 0.02 us -> 338 us  [per_device(): cols_weight = lax.all_gather(mixed_own, ('blk', 'grp'), axis=1, tiled=True)]
  transfers between devices with their start and end apart: 2 -> 3, of which waited for: 0 -> 1; matrix products, arithmetic and copies ran while one was open for 1% -> 2% of each run, Pallas kernels for 0% -> 0%
where the time goes in v1:
time: 1200 us
  blocking collectives  744 us (62%)
  waiting for transfers between devices  339 us (28%)
  matrix products  73 us (6%)
  between operations  14.9 us (1%)
  starting transfers between devices  13.6 us (1%)
    all_gather x1, blocking collectives, per_device(): lax.all_gather(high_probes, ('blk', 'grp'), axis=1, tiled=True)  628 us
    all_gather x1, waiting for transfers between devices, per_device(): cols_weight = lax.all_gather(mixed_own, ('blk', 'grp'), axis=1, tiled=True)  338 us
    dot_general x24, matrix products, matern(): inner = jnp.einsum('fr,fc->rc', rows, cols, precision=lax.Precision.HIGHEST)  40.2 us
    all_gather x1, blocking collectives, per_device(): lax.all_gather(low_sites, 'grp', axis=1, tiled=True)  34.5 us
    all_gather x1, blocking collectives, per_device(): lax.all_gather(high_probes, 'grp', axis=1, tiled=True)  34.4 us
    all_gather x1, blocking collectives, per_device(): low_block = lax.all_gather(new_low, 'grp', axis=1, tiled=True)  34.3 us
    dot_general x24, matrix products, partial_product(): jnp.einsum('pc,rc->pr', weights, tile, precision=lax.Precision.HIGHEST)  30.7 us
  transfers between devices with their start and end apart: 3, of which 1 were waited for; matrix products, arithmetic and copies ran while one was open for 2% of the time, Pallas kernels for 0%

profile of v1, /device:TPU:128, one launch (start us, length us, event | category | flops | bytes accessed | tf_op | source)
XLA Modules:
  0.0 1197.8 jit_solution(416046895081307881)
XLA Ops:
  8.6 34.5 %all_gather.27 = f32[8,1024]{1,0:T(8,128)S(1)} all-gather(f32[8,128]{1,0:T(8,128)S(1)} %copy-done), channel_id=1, replica_groups=mesh['blk'=32,'grp'=8] {'grp'}, dimensions={1}, use_global_device_ids=true | all-gather | bytes 36864 | tf_op jit(solution)/shard_map/all_gather | solution.py:42
  45.6 13.5 %all-to-all-start = ((f32[256,1,512]{2,1,0:T(1,128)}), f32[256,1,512]{2,1,0:T(1,128)S(1)}, u32[]{:S(2)}, u32[]{:S(2)}) async-start(f32[256,1,512]{2,1,0:T(1,128)} %reshape.54), calls=%async_computation | async-start | bytes 1048576 | tf_op jit(solution)/shard_map/all_to_all | solution.py:66
  59.1 34.4 %all-gather = f32[8,64,8]{1,2,0:T(8,128)S(1)} all-gather(f32[1,64,8]{1,2,0:T(8,128)S(1)} %bitcast.93), channel_id=1, replica_groups=mesh['blk'=32,'grp'=8] {'grp'}, dimensions={0}, use_global_device_ids=true | all-gather | bytes 18432 | tf_op jit(solution)/shard_map/all_gather | solution.py:44
  95.8 12.6 %all-reduce = s32[512]{0:T(512)S(1)} all-reduce(s32[512]{0:T(512)S(1)} %dynamic-update-slice), channel_id=1, replica_groups=mesh['blk'=32,'grp'=8] {'grp'}, use_global_device_ids=true, to_apply=%add | all-reduce | flops 512 | bytes 4096
  110.0 628.1 %all-gather.1 = f32[256,64,8]{1,2,0:T(8,128)S(1)} all-gather(f32[1,64,8]{1,2,0:T(8,128)S(1)} %bitcast.94), channel_id=1, replica_groups=mesh['blk'=32,'grp'=8] {'blk','grp'}, dimensions={0}, use_global_device_ids=true | all-gather | bytes 526336 | tf_op jit(solution)/shard_map/all_gather | solution.py:71
  742.8 12.1 %while.27 = (s32[]{:T(128)}, f32[8,64]{1,0:T(8,128)S(1)}, f32[8,8,2048]{2,0,1:T(8,128)S(1)}, f32[64]{0:T(128)S(1)}, f32[8,8,2048]{2,0,1:T(8,128)S(1)}, /*index=5*/f32[8,64]{1,0:T(8,128)S(1)}, s32[]{:T(128)}, s32[]{:T(128)}) while((s32[]{:T(128)}, f32[8,64]{1,0:T(8,128)S(1)}, f32[8,8,2048]{2,0,1:T(8,128)S(1)}, f32[64]{0:T(128)S(1)}, ...), condition=%wide.region_7.8_spmd.clone, body=%wide.region_5.0_spmd.clone.sunk | while | flops 26246148 | bytes 1530219 | solution.py:35
  756.3 338.1 %all-gather.5.cloned.1.call-done = f32[8,32768]{1,0:T(8,128)} async-done(((f32[8,128]{1,0:T(8,128)}), f32[8,32768]{1,0:T(8,128)}) %all-gather.5.cloned.1.call-update) | async-done | bytes 1048592 | tf_op jit(solution)/shard_map/all_gather | solution.py:64
  1094.4 61.4 %while.26 = (s32[]{:T(128)}, f32[8,128]{1,0:T(8,128)S(1)}, f32[16,8,2048]{2,1,0:T(8,128)}, f32[128]{0:T(128)S(1)}, f32[16,8,2048]{2,1,0:T(8,128)S(1)}, /*index=5*/f32[8,128]{1,0:T(8,128)S(1)}, s32[]{:T(128)}, s32[]{:T(128)}) while((s32[]{:T(128)}, f32[8,128]{1,0:T(8,128)S(1)}, f32[16,8,2048]{2,1,0:T(8,128)}, f32[128]{0:T(128)S(1)}, ...), condition=%wide.region_3.4_spmd.clone, body=%wide.region_1.3_spmd.clone.sunk | while | flops 52461568 | bytes 2323059 | solution.py:35
  1094.4 2.1 fusion.64
  1098.2 2.1 fusion.64
  1102.1 2.1 fusion.64
  1105.9 2.1 fusion.64
  1109.8 2.1 fusion.64
  1113.6 2.1 fusion.64
  1117.4 2.1 fusion.64
  1121.3 2.1 fusion.64
  1125.1 2.1 fusion.64
  1129.0 2.1 fusion.64
  1132.8 2.1 fusion.64
  1136.7 2.1 fusion.64
  1140.5 2.1 fusion.64
  1144.3 2.1 fusion.64
  1148.2 2.1 fusion.64
  1155.8 34.3 %all_gather.25 = f32[8,1024]{1,0:T(8,128)S(1)} all-gather(f32[8,128]{1,0:T(8,128)S(1)} %get-tuple-element.132), channel_id=1, replica_groups=mesh['blk'=32,'grp'=8] {'grp'}, dimensions={1}, use_global_device_ids=true | all-gather | bytes 36864 | tf_op jit(solution)/shard_map/all_gather | solution.py:75
  (113 shorter events, 54.6 us)
Async XLA Ops:
  7.2 747.7 %all-gather.7.cloned.1.call-start = ((), (), s32[]{:S(2)}) async-start(), calls=%async_computation.2 | async-start | bytes 1052672 | tf_op jit(solution)/shard_map/all_gather | solution.py:63
  7.9 0.7 copy-start
  8.6 34.5 %copy-start.6 = (s32[64]{0:T(128)S(1)}, s32[64]{0:T(128)}, u32[]{:S(2)}) copy-start(s32[64]{0:T(128)} %param.13) | copy-start | bytes 772
  43.1 0.7 copy-start.4
  45.6 13.5 %copy-start.1 = (f32[8,64]{1,0:T(8,128)S(1)}, f32[8,64]{1,0:T(8,128)}, u32[]{:S(2)}) copy-start(f32[8,64]{1,0:T(8,128)} %param.12) | copy-start | bytes 6148
  45.6 693.9 %all-to-all-start = ((f32[256,1,512]{2,1,0:T(1,128)}), f32[256,1,512]{2,1,0:T(1,128)S(1)}, u32[]{:S(2)}, u32[]{:S(2)}) async-start(f32[256,1,512]{2,1,0:T(1,128)} %reshape.54), calls=%async_computation | async-start | bytes 1048576 | tf_op jit(solution)/shard_map/all_to_all | solution.py:66
  59.0 1035.3 %all-gather.5.cloned.1.call-start = ((), (), s32[]{:S(2)}) async-start(), calls=%async_computation.1 | async-start | bytes 1052672 | tf_op jit(solution)/shard_map/all_gather | solution.py:64
  93.6 0.7 copy-start.7
  108.4 0.7 copy-start.5
  738.7 0.7 copy-start.3
  1155.8 34.3 %copy-start.2 = (f32[8,128]{1,0:T(8,128)}, f32[8,128]{1,0:T(8,128)S(1)}, u32[]{:S(2)}) copy-start(f32[8,128]{1,0:T(8,128)S(1)} %get-tuple-element.132) | copy-start | bytes 12292
Sparse Core Ops, SparseCore 0:
  9.8 546.4 all-gather.6
  558.6 535.6 all-gather.4
